TPU v7x, 128 devices: a whole 4x4x4 slice. The times are simulated.
128 devices in a mesh: seq: 32 (over y, x, core), mp: 4 (over z).
Axes of the slice: x: 4, y: 4, z: 4, core: 2. Of those that a mesh axis runs over, the one named last changes fastest.
Arguments:
- states: bfloat16 [4, 16, 2048], P(None, None, 'mp'), may hold values from -4 to 4
- query_weight: bfloat16 [2048, 2048], P('seq', 'mp'), may hold values from -5 to 5
- key_weight: bfloat16 [2048, 2048], P('seq', 'mp'), may hold values from -5 to 5
- value_weight: bfloat16 [2048, 2048], P('seq', 'mp'), may hold values from -5 to 5
- output_weight: bfloat16 [2048, 2048], P('seq', 'mp'), may hold values from -5 to 5
- gate_weight: bfloat16 [2048, 8192], P('seq', 'mp'), may hold values from -5 to 5
- up_weight: bfloat16 [2048, 8192], P('seq', 'mp'), may hold values from -5 to 5
- down_weight: bfloat16 [8192, 2048], P('seq', 'mp'), may hold values from -5 to 5
- query_gain: float32 [2048], P('mp'), may hold values from 0.5 to 2
- key_gain: float32 [2048], P('mp'), may hold values from 0.5 to 2
- attention_gain: float32 [2048], P('mp'), may hold values from 0.1 to 1.9
- feedforward_gain: float32 [2048], P('mp'), may hold values from 0.1 to 1.9
- key_cache: bfloat16 [512, 256, 2048], P('seq', None, 'mp'), may hold values from -500 to 500
- value_cache: bfloat16 [512, 256, 2048], P('seq', None, 'mp'), may hold values from -6 to 6
- lengths: int32 [16], replicated, may hold values from 1 to 32768, as said below
- page_owner: int32 [512], P('seq'), may hold values from -1 to 15, as said below
- page_index: int32 [512], P('seq'), may hold values from 0 to 127, as said below
Outputs:
- decoded: bfloat16 [4, 16, 2048], P(None, None, 'mp')
Inputs may be any that keep to these rules, and one draw needn't show every extreme that they name: Request r owns exactly ceil(lengths[r] / 256) pages. `page_owner`: on each device of seq the used pages come before the unused ones. `page_index`: the pages of one request carry the numbers 0, 1, 2 and so on, once each; unused pages carry 0.
All inputs are finite; a program needn't handle non-finite values.
Results may differ from a plain program's by a relative error of at most 0.015.
Values may be sent and summed in bfloat16 or wider, within the bound.
No kernel may reach another device: no remote copies, remote signals or barrier semaphores. Data moves between devices by JAX's collectives and lax.ppermute only.
A program may use at most 64 MiB of HBM per device.

v0:
```python
import jax
import jax.numpy as jnp
from jax import lax
from jax.sharding import PartitionSpec as P

D = 2048
HD = 128
R = 16
STEPS = 4
PAGE = 256
epsilon = 1e-06
rope_base = 500000.0
very_low = -1e30
exact_mode = lax.Precision.HIGHEST
pages_per_block = 4


def combined_all(value, axis, join):
    pieces = jax.tree.map(lambda part: lax.all_gather(part, axis), value)
    head = jax.tree.map(lambda part: part[0], pieces)
    tail = jax.tree.map(lambda part: part[1:], pieces)
    subtotal, _ = lax.scan(lambda subtotal, piece: (join(subtotal, piece), None), head, tail)
    return subtotal


def rotary(values, positions):
    half_width = HD // 2
    frequencies = rope_base ** (-2.0 * jnp.arange(half_width, dtype=jnp.float32) / HD)
    angles = positions.astype(jnp.float32)[:, None] * frequencies[None, :]
    cosine = jnp.cos(angles)[:, None, :]
    sine_part = jnp.sin(angles)[:, None, :]
    first_half = values[..., :half_width]
    second_half = values[..., half_width:]
    return jnp.concatenate(
        [
            first_half * cosine - second_half * sine_part,
            second_half * cosine + first_half * sine_part,
        ],
        axis=-1,
    )


def seq_columns(token_rows, width):
    gathered = lax.all_gather(token_rows, "mp", axis=1, tiled=True)
    return lax.dynamic_slice_in_dim(gathered, lax.axis_index("seq") * width, width, 1)


def seq_total(partial_value):
    return lax.psum(partial_value, "seq")


def feature_sums(squares):
    return lax.psum(squares, "mp")


def inverse_rms(square_total):
    return lax.rsqrt(square_total / D + epsilon)[:, None]


def combine_parts(earlier, later_part):
    highest = jnp.maximum(earlier[0], later_part[0])
    first_scale = jnp.exp(earlier[0] - highest)
    second_scale = jnp.exp(later_part[0] - highest)
    return (
        highest,
        earlier[1] * first_scale + later_part[1] * second_scale,
        earlier[2] * first_scale[..., None] + later_part[2] * second_scale[..., None],
    )


def local(
    states,
    query_weight,
    key_weight,
    value_weight,
    output_weight,
    gate_weight,
    up_weight,
    down_weight,
    query_gain,
    key_gain,
    attention_gain,
    feedforward_gain,
    key_cache,
    value_cache,
    lengths,
    page_owner,
    page_index,
):
    local_width = query_weight.shape[1]
    local_heads = local_width // HD
    requests = jnp.arange(R, dtype=jnp.int32)
    score_scale = HD ** (-0.5)
    outputs = []
    key_list = []
    value_list = []
    for step_index in range(STEPS):
        token_rows = states[step_index]
        positions = lengths + step_index
        attention_row_count = token_rows.shape[0]
        attention_sliced = seq_columns(token_rows, query_weight.shape[0])
        partial_value = jnp.concatenate(
            [
                jnp.dot(attention_sliced, query_weight, preferred_element_type=jnp.float32),
                jnp.dot(attention_sliced, key_weight, preferred_element_type=jnp.float32),
                jnp.dot(attention_sliced, value_weight, preferred_element_type=jnp.float32),
            ],
            axis=1,
        )
        summed = seq_total(partial_value)
        query_raw = summed[:, :local_width]
        key_raw = summed[:, local_width : 2 * local_width]
        value_raw = summed[:, 2 * local_width :]
        squares = feature_sums(
            jnp.stack(
                [jnp.sum(query_raw * query_raw, axis=1), jnp.sum(key_raw * key_raw, axis=1)], axis=1
            )
        )
        attention_queries = query_raw * inverse_rms(squares[:, 0]) * query_gain
        attention_new_keys = key_raw * inverse_rms(squares[:, 1]) * key_gain
        attention_queries = rotary(
            attention_queries.reshape(attention_row_count, local_heads, HD), positions
        ).astype(jnp.bfloat16)
        attention_new_keys = rotary(
            attention_new_keys.reshape(attention_row_count, local_heads, HD), positions
        ).astype(jnp.bfloat16)
        attention_new_values = value_raw.astype(jnp.bfloat16).reshape(
            attention_row_count, local_heads, HD
        )
        key_list.append(attention_new_keys[None])
        value_list.append(attention_new_values[None])
        cache_queries = attention_queries[None]
        steps_here = cache_queries.shape[0]

        def fold_block(block_index, carried):
            maxima, totals, running = carried
            first_page = block_index * pages_per_block
            key_block = lax.dynamic_slice_in_dim(key_cache, first_page, pages_per_block, 0).reshape(
                pages_per_block, PAGE, local_heads, HD
            )
            value_block = lax.dynamic_slice_in_dim(
                value_cache, first_page, pages_per_block, 0
            ).reshape(pages_per_block, PAGE, local_heads, HD)
            owners = lax.dynamic_slice_in_dim(page_owner, first_page, pages_per_block, 0)
            indices = lax.dynamic_slice_in_dim(page_index, first_page, pages_per_block, 0)
            matches = owners[:, None] == requests[None, :]
            onehot = matches.astype(jnp.float32)
            picked = jnp.take(cache_queries, jnp.maximum(owners, 0), axis=1)
            scores = (
                jnp.einsum("sghd,gthd->sgth", picked, key_block, preferred_element_type=jnp.float32)
                * score_scale
            )
            page_lengths = jnp.sum(jnp.where(matches, lengths[None, :], 0), axis=1)
            token_spots = indices[:, None] * PAGE + jnp.arange(PAGE, dtype=jnp.int32)[None, :]
            validity = (token_spots < page_lengths[:, None])[None, :, :, None]
            masked = jnp.where(validity, scores, very_low)
            page_top = jnp.max(masked, axis=2)
            request_top = jnp.max(
                jnp.where(matches.T[None, :, :, None], page_top[:, None, :, :], very_low), axis=2
            )
            highest = jnp.maximum(maxima, request_top)
            page_ref = jnp.take(highest, jnp.maximum(owners, 0), axis=1)
            weights = jnp.where(validity, jnp.exp(masked - page_ref[:, :, None, :]), 0.0)
            page_total = jnp.sum(weights, axis=2)
            page_sum = jnp.einsum(
                "sgth,gthd->sghd",
                weights.astype(jnp.bfloat16),
                value_block,
                preferred_element_type=jnp.float32,
            )
            factor = jnp.exp(maxima - highest)
            totals = totals * factor + jnp.einsum(
                "gr,sgh->srh", onehot, page_total, precision=exact_mode
            )
            running = running * factor[..., None] + jnp.einsum(
                "gr,sghd->srhd", onehot, page_sum, precision=exact_mode
            )
            return (highest, totals, running)

        block_count = page_owner.shape[0] // pages_per_block
        initial = (
            jnp.full((steps_here, R, local_heads), very_low, jnp.float32),
            jnp.zeros((steps_here, R, local_heads), jnp.float32),
            jnp.zeros((steps_here, R, local_heads, HD), jnp.float32),
        )
        maxima, totals, running = lax.fori_loop(0, block_count, fold_block, initial)
        merged_parts = combined_all((maxima, totals, running), "seq", combine_parts)
        finish_queries = attention_queries[None]
        finish_new_keys = jnp.concatenate(key_list, axis=0)
        finish_maxima, finish_totals, finish_running = merged_parts
        finish_steps_here = finish_queries.shape[0]
        known = finish_new_keys.shape[0]
        fresh_scores = (
            jnp.einsum(
                "srhd,trhd->srht",
                finish_queries,
                finish_new_keys,
                preferred_element_type=jnp.float32,
            )
            * score_scale
        )
        allowed = (
            jnp.arange(known)[None, :] <= step_index + jnp.arange(finish_steps_here)[:, None]
        )[:, None, None, :]
        fresh_scores = jnp.where(allowed, fresh_scores, very_low)
        finish_highest = jnp.maximum(finish_maxima, jnp.max(fresh_scores, axis=-1))
        fresh_weights = jnp.where(allowed, jnp.exp(fresh_scores - finish_highest[..., None]), 0.0)
        finish_factor = jnp.exp(finish_maxima - finish_highest)
        finish_totals = finish_totals * finish_factor + jnp.sum(fresh_weights, axis=-1)
        finish_running = finish_running * finish_factor[..., None] + jnp.einsum(
            "srht,trhd->srhd",
            fresh_weights.astype(jnp.bfloat16),
            jnp.concatenate(value_list, axis=0),
            preferred_element_type=jnp.float32,
        )
        attended = (finish_running / finish_totals[..., None]).astype(jnp.bfloat16)
        layer_attended = attended.reshape(R, local_width)
        sliced = seq_columns(layer_attended, output_weight.shape[0])
        attention_out = seq_total(
            jnp.dot(sliced, output_weight, preferred_element_type=jnp.float32)
        )
        attention_squares = feature_sums(
            jnp.sum(attention_out * attention_out, axis=1, keepdims=True)
        )
        hidden = (
            token_rows.astype(jnp.float32)
            + attention_out * inverse_rms(attention_squares[:, 0]) * attention_gain
        ).astype(jnp.bfloat16)
        hidden_cols = seq_columns(hidden, gate_weight.shape[0])
        gate_part = jnp.dot(hidden_cols, gate_weight, preferred_element_type=jnp.float32)
        up_part = jnp.dot(hidden_cols, up_weight, preferred_element_type=jnp.float32)
        hidden_units = gate_weight.shape[1]
        summed_both = seq_total(jnp.concatenate([gate_part, up_part], axis=1))
        active = (
            jax.nn.silu(summed_both[:, :hidden_units]) * summed_both[:, hidden_units:]
        ).astype(jnp.bfloat16)
        active_cols = seq_columns(active, down_weight.shape[0])
        mlp_out = seq_total(jnp.dot(active_cols, down_weight, preferred_element_type=jnp.float32))
        mlp_squares = feature_sums(jnp.sum(mlp_out * mlp_out, axis=1, keepdims=True))
        outputs.append(
            (
                hidden.astype(jnp.float32)
                + mlp_out * inverse_rms(mlp_squares[:, 0]) * feedforward_gain
            ).astype(jnp.bfloat16)
        )
    return jnp.stack(outputs, axis=0)


def solution(mesh):
    in_specs = (
        P(None, None, "mp"),
        P("seq", "mp"),
        P("seq", "mp"),
        P("seq", "mp"),
        P("seq", "mp"),
        P("seq", "mp"),
        P("seq", "mp"),
        P("seq", "mp"),
        P("mp"),
        P("mp"),
        P("mp"),
        P("mp"),
        P("seq", None, "mp"),
        P("seq", None, "mp"),
        P(),
        P("seq"),
        P("seq"),
    )
    out_specs = P(None, None, "mp")
    return jax.shard_map(local, mesh=mesh, in_specs=in_specs, out_specs=out_specs, check_vma=False)
```

profile of v0, /device:TPU:6, one launch (start us, length us, event | category | flops | bytes accessed | tf_op | source)
XLA Modules:
  0.0 1058.9 jit_solution(6257620773819369397)
XLA Ops:
  7.4 13.1 %all-gather = bf16[1,16,2048]{2,1,0:T(8,128)(2,1)S(1)} all-gather(bf16[1,16,512]{2,1,0:T(8,128)(2,1)S(1)} %get-tuple-element.1524), channel_id=2, replica_groups=mesh['seq'=32,'mp'=4] {'mp'}, dimensions={2}, use_global_device_ids=true | all-gather | bytes 81920 | tf_op jit(solution)/shard_map/all_gather | solution.py:44
  72.1 104.6 %all-reduce.18.cloned.1.call-done = (f32[16,1536]{1,0:T(8,128)}, f32[16,1536]{1,0:T(8,128)}, f32[16,1536]{1,0:T(8,128)}, f32[16,1536]{1,0:T(8,128)}) async-done(((f32[16,1536]{1,0:T(8,128)}, f32[16,1536]{1,0:T(8,128)}, f32[16,1536]{1,0:T(8,128)}, f32[16,1536]{1,0:T(8,128)}), (f32[16,1536]{1,0:T(8,128)}, f32[16,1536]{1,0:T(8,128)}, f32[16,1536]{1,0:T(8,128)}, ...) | async-done | bytes 393232 | tf_op jit(solution)/shard_map/psum | solution.py:49
  190.7 26.4 %while.139 = (s32[]{:T(128)}, f32[1,16,4]{1,2,0:T(4,128)S(1)}, f32[1,16,4]{1,2,0:T(4,128)S(1)}, f32[1,16,4,128]{3,1,2,0:T(8,128)S(1)}, s32[16]{0:T(128)S(1)}, /*...) while((s32[]{:T(128)}, f32[1,16,4]{1,2,0:T(4,128)S(1)}, ...), condition=%wide.region_70.73_spmd.clone.clone, body=%wide.region_65.72_spmd.clone.clone.sunk | while | flops 2561347 | bytes 6471395 | solution.py:186
  218.1 26.4 %while.138 = (s32[]{:T(128)}, f32[1,16,4]{1,2,0:T(4,128)S(1)}, f32[1,16,4]{1,2,0:T(4,128)S(1)}, f32[1,16,4,128]{3,1,2,0:T(8,128)S(1)}, s32[16]{0:T(128)S(1)}, /*...) while((s32[]{:T(128)}, f32[1,16,4]{1,2,0:T(4,128)S(1)}, ...), condition=%wide.region_49.52_spmd.clone.clone, body=%wide.region_44.51_spmd.clone.clone.sunk | while | flops 2561347 | bytes 6471395 | solution.py:186
  245.1 26.3 %while.137 = (s32[]{:T(128)}, f32[1,16,4]{1,2,0:T(4,128)S(1)}, f32[1,16,4]{1,2,0:T(4,128)S(1)}, f32[1,16,4,128]{3,1,2,0:T(8,128)S(1)}, s32[16]{0:T(128)S(1)}, /*...) while((s32[]{:T(128)}, f32[1,16,4]{1,2,0:T(4,128)S(1)}, ...), condition=%wide.region_28.31_spmd.clone.clone, body=%wide.region_23.30_spmd.clone.clone.sunk | while | flops 2561347 | bytes 6471395 | solution.py:186
  272.0 26.4 %while.136 = (s32[]{:T(128)}, f32[1,16,4]{1,2,0:T(4,128)S(1)}, f32[1,16,4]{1,2,0:T(4,128)S(1)}, f32[1,16,4,128]{3,1,2,0:T(8,128)S(1)}, s32[16]{0:T(128)S(1)}, /*...) while((s32[]{:T(128)}, f32[1,16,4]{1,2,0:T(4,128)S(1)}, ...), condition=%wide.region_9.12_spmd.clone.clone, body=%wide.region_4.11_spmd.clone.clone.sunk | while | flops 2561347 | bytes 6471395 | solution.py:186
  301.5 21.3 %all-gather.13 = f32[32,16,4]{1,2,0:T(4,128)S(1)} all-gather(f32[1,16,4]{1,2,0:T(4,128)S(1)} %get-tuple-element.937), channel_id=15, replica_groups=mesh['seq'=32,'mp'=4] {'seq'}, dimensions={0}, use_global_device_ids=true | all-gather | bytes 8448 | tf_op jit(solution)/shard_map/all_gather | solution.py:19
  322.8 24.2 %all-gather.14 = f32[32,16,4]{1,2,0:T(4,128)S(1)} all-gather(f32[1,16,4]{1,2,0:T(4,128)S(1)} %get-tuple-element.938), channel_id=16, replica_groups=mesh['seq'=32,'mp'=4] {'seq'}, dimensions={0}, use_global_device_ids=true | all-gather | bytes 8448 | tf_op jit(solution)/shard_map/all_gather | solution.py:19
  347.6 21.6 %all-gather.9 = f32[32,16,4]{1,2,0:T(4,128)S(1)} all-gather(f32[1,16,4]{1,2,0:T(4,128)S(1)} %get-tuple-element.931), channel_id=11, replica_groups=mesh['seq'=32,'mp'=4] {'seq'}, dimensions={0}, use_global_device_ids=true | all-gather | bytes 8448 | tf_op jit(solution)/shard_map/all_gather | solution.py:19
  369.2 24.0 %all-gather.10 = f32[32,16,4]{1,2,0:T(4,128)S(1)} all-gather(f32[1,16,4]{1,2,0:T(4,128)S(1)} %get-tuple-element.932), channel_id=12, replica_groups=mesh['seq'=32,'mp'=4] {'seq'}, dimensions={0}, use_global_device_ids=true | all-gather | bytes 8448 | tf_op jit(solution)/shard_map/all_gather | solution.py:19
  393.7 21.6 %all-gather.5 = f32[32,16,4]{1,2,0:T(4,128)S(1)} all-gather(f32[1,16,4]{1,2,0:T(4,128)S(1)} %get-tuple-element.925), channel_id=7, replica_groups=mesh['seq'=32,'mp'=4] {'seq'}, dimensions={0}, use_global_device_ids=true | all-gather | bytes 8448 | tf_op jit(solution)/shard_map/all_gather | solution.py:19
  415.3 24.0 %all-gather.6 = f32[32,16,4]{1,2,0:T(4,128)S(1)} all-gather(f32[1,16,4]{1,2,0:T(4,128)S(1)} %get-tuple-element.926), channel_id=8, replica_groups=mesh['seq'=32,'mp'=4] {'seq'}, dimensions={0}, use_global_device_ids=true | all-gather | bytes 8448 | tf_op jit(solution)/shard_map/all_gather | solution.py:19
  439.8 21.6 %all-gather.1 = f32[32,16,4]{1,2,0:T(4,128)S(1)} all-gather(f32[1,16,4]{1,2,0:T(4,128)S(1)} %get-tuple-element.919), channel_id=3, replica_groups=mesh['seq'=32,'mp'=4] {'seq'}, dimensions={0}, use_global_device_ids=true | all-gather | bytes 8448 | tf_op jit(solution)/shard_map/all_gather | solution.py:19
  461.3 24.0 %all-gather.2 = f32[32,16,4]{1,2,0:T(4,128)S(1)} all-gather(f32[1,16,4]{1,2,0:T(4,128)S(1)} %get-tuple-element.920), channel_id=4, replica_groups=mesh['seq'=32,'mp'=4] {'seq'}, dimensions={0}, use_global_device_ids=true | all-gather | bytes 8448 | tf_op jit(solution)/shard_map/all_gather | solution.py:19
  488.8 12.3 %while.135 = (s32[]{:T(128)}, f32[1,16,4]{1,2,0:T(4,128)S(1)}, f32[1,16,4]{1,2,0:T(4,128)S(1)}, f32[1,16,4,128]{3,2,1,0:T(4,128)S(1)}, f32[31,1,16,4]{2,3,1,0:T(...) while((s32[]{:T(128)}, f32[1,16,4]{1,2,0:T(4,128)S(1)}, ...), condition=%wide.region_72.75_spmd, body=%wide.region_71.74_spmd.sunk | while | flops 25026 | bytes 168809 | solution.py:22
  503.6 12.3 %while.134 = (s32[]{:T(128)}, f32[1,16,4]{1,2,0:T(4,128)S(1)}, f32[1,16,4]{1,2,0:T(4,128)S(1)}, f32[1,16,4,128]{3,2,1,0:T(4,128)S(1)}, f32[31,1,16,4]{2,3,1,0:T(...) while((s32[]{:T(128)}, f32[1,16,4]{1,2,0:T(4,128)S(1)}, ...), condition=%wide.region_51.54_spmd, body=%wide.region_50.53_spmd.sunk | while | flops 25026 | bytes 168809 | solution.py:22
  527.6 12.3 %while.133 = (s32[]{:T(128)}, f32[1,16,4]{1,2,0:T(4,128)S(1)}, f32[1,16,4]{1,2,0:T(4,128)S(1)}, f32[1,16,4,128]{3,2,1,0:T(4,128)S(1)}, f32[31,1,16,4]{2,3,1,0:T(...) while((s32[]{:T(128)}, f32[1,16,4]{1,2,0:T(4,128)S(1)}, ...), condition=%wide.region_30.33_spmd, body=%wide.region_29.32_spmd.sunk | while | flops 25026 | bytes 168809 | solution.py:22
  541.5 12.3 %all_gather.157 = bf16[16,2048]{1,0:T(8,128)(2,1)S(1)} all-gather(bf16[16,512]{1,0:T(8,128)(2,1)S(1)} %bitcast.1038), channel_id=1, replica_groups=mesh['seq'=32,'mp'=4] {'mp'}, dimensions={1}, use_global_device_ids=true | all-gather | bytes 81920 | tf_op jit(solution)/shard_map/all_gather | solution.py:44
  553.8 11.9 %all_gather.147 = bf16[16,2048]{1,0:T(8,128)(2,1)S(1)} all-gather(bf16[16,512]{1,0:T(8,128)(2,1)S(1)} %bitcast.1039), channel_id=1, replica_groups=mesh['seq'=32,'mp'=4] {'mp'}, dimensions={1}, use_global_device_ids=true | all-gather | bytes 81920 | tf_op jit(solution)/shard_map/all_gather | solution.py:44
  581.9 12.3 %while.132 = (s32[]{:T(128)}, f32[1,16,4]{1,2,0:T(4,128)S(1)}, f32[1,16,4]{1,2,0:T(4,128)S(1)}, f32[1,16,4,128]{3,2,1,0:T(4,128)S(1)}, f32[31,1,16,4]{2,3,1,0:T(...) while((s32[]{:T(128)}, f32[1,16,4]{1,2,0:T(4,128)S(1)}, ...), condition=%wide.region_11.14_spmd, body=%wide.region_10.13_spmd.sunk | while | flops 25026 | bytes 168809 | solution.py:22
  594.7 11.9 %all_gather.127 = bf16[16,2048]{1,0:T(8,128)(2,1)S(1)} all-gather(bf16[16,512]{1,0:T(8,128)(2,1)S(1)} %bitcast.1041), channel_id=1, replica_groups=mesh['seq'=32,'mp'=4] {'mp'}, dimensions={1}, use_global_device_ids=true | all-gather | bytes 81920 | tf_op jit(solution)/shard_map/all_gather | solution.py:44
  607.4 101.3 %all-reduce.14.cloned.1.call-done = (f32[16,512]{1,0:T(8,128)}, f32[16,512]{1,0:T(8,128)}, f32[16,512]{1,0:T(8,128)}, f32[16,512]{1,0:T(8,128)}) async-done(((f32[16,512]{1,0:T(8,128)}, f32[16,512]{1,0:T(8,128)}, f32[16,512]{1,0:T(8,128)}, f32[16,512]{1,0:T(8,128)}), (f32[16,512]{1,0:T(8,128)}, f32[16,512]{1,0:T(8,128)}, f32[16,512]{1,0:T(8,128)}, f32[16,512]{1,0:T(8,128)})) %all-reduce.14.cloned.1.call-update) | async-done | bytes 131088 | tf_op jit(solution)/shard_map/psum | solution.py:49
  723.9 11.9 %all_gather.158 = bf16[16,2048]{1,0:T(8,128)(2,1)S(1)} all-gather(bf16[16,512]{1,0:T(8,128)(2,1)S(1)} %get-tuple-element.1522), channel_id=1, replica_groups=mesh['seq'=32,'mp'=4] {'mp'}, dimensions={1}, use_global_device_ids=true | all-gather | bytes 81920 | tf_op jit(solution)/shard_map/all_gather | solution.py:44
  736.2 11.9 %all_gather.148 = bf16[16,2048]{1,0:T(8,128)(2,1)S(1)} all-gather(bf16[16,512]{1,0:T(8,128)(2,1)S(1)} %get-tuple-element.1521), channel_id=1, replica_groups=mesh['seq'=32,'mp'=4] {'mp'}, dimensions={1}, use_global_device_ids=true | all-gather | bytes 81920 | tf_op jit(solution)/shard_map/all_gather | solution.py:44
  748.5 11.9 %all_gather.138 = bf16[16,2048]{1,0:T(8,128)(2,1)S(1)} all-gather(bf16[16,512]{1,0:T(8,128)(2,1)S(1)} %get-tuple-element.1520), channel_id=1, replica_groups=mesh['seq'=32,'mp'=4] {'mp'}, dimensions={1}, use_global_device_ids=true | all-gather | bytes 81920 | tf_op jit(solution)/shard_map/all_gather | solution.py:44
  760.8 12.0 %all_gather.128 = bf16[16,2048]{1,0:T(8,128)(2,1)S(1)} all-gather(bf16[16,512]{1,0:T(8,128)(2,1)S(1)} %get-tuple-element.1519), channel_id=1, replica_groups=mesh['seq'=32,'mp'=4] {'mp'}, dimensions={1}, use_global_device_ids=true | all-gather | bytes 81920 | tf_op jit(solution)/shard_map/all_gather | solution.py:44
  776.3 103.1 %all-reduce.16.cloned.1.call-done = (f32[16,4096]{1,0:T(8,128)}, f32[16,4096]{1,0:T(8,128)}, f32[16,4096]{1,0:T(8,128)}, f32[16,4096]{1,0:T(8,128)}) async-done(((f32[16,4096]{1,0:T(8,128)}, f32[16,4096]{1,0:T(8,128)}, f32[16,4096]{1,0:T(8,128)}, f32[16,4096]{1,0:T(8,128)}), (f32[16,4096]{1,0:T(8,128)}, f32[16,4096]{1,0:T(8,128)}, f32[16,4096]{1,0:T(8,128)}, ...) | async-done | bytes 1048592 | tf_op jit(solution)/shard_map/psum | solution.py:49
  880.4 13.0 %all_gather.159 = bf16[16,8192]{1,0:T(8,128)(2,1)S(1)} all-gather(bf16[16,2048]{1,0:T(8,128)(2,1)S(1)} %fusion.120), channel_id=1, replica_groups=mesh['seq'=32,'mp'=4] {'mp'}, dimensions={1}, use_global_device_ids=true | all-gather | bytes 327680 | tf_op jit(solution)/shard_map/all_gather | solution.py:44
  894.4 12.3 %all_gather.149 = bf16[16,8192]{1,0:T(8,128)(2,1)S(1)} all-gather(bf16[16,2048]{1,0:T(8,128)(2,1)S(1)} %fusion.121), channel_id=1, replica_groups=mesh['seq'=32,'mp'=4] {'mp'}, dimensions={1}, use_global_device_ids=true | all-gather | bytes 327680 | tf_op jit(solution)/shard_map/all_gather | solution.py:44
  909.2 12.3 %all_gather.139 = bf16[16,8192]{1,0:T(8,128)(2,1)S(1)} all-gather(bf16[16,2048]{1,0:T(8,128)(2,1)S(1)} %fusion.122), channel_id=1, replica_groups=mesh['seq'=32,'mp'=4] {'mp'}, dimensions={1}, use_global_device_ids=true | all-gather | bytes 327680 | tf_op jit(solution)/shard_map/all_gather | solution.py:44
  923.3 12.3 %all_gather.129 = bf16[16,8192]{1,0:T(8,128)(2,1)S(1)} all-gather(bf16[16,2048]{1,0:T(8,128)(2,1)S(1)} %fusion.123), channel_id=1, replica_groups=mesh['seq'=32,'mp'=4] {'mp'}, dimensions={1}, use_global_device_ids=true | all-gather | bytes 327680 | tf_op jit(solution)/shard_map/all_gather | solution.py:44
  936.3 100.0 %all-reduce.12.cloned.1.call-done = (f32[16,512]{1,0:T(8,128)}, f32[16,512]{1,0:T(8,128)}, f32[16,512]{1,0:T(8,128)}, f32[16,512]{1,0:T(8,128)}) async-done(((f32[16,512]{1,0:T(8,128)}, f32[16,512]{1,0:T(8,128)}, f32[16,512]{1,0:T(8,128)}, f32[16,512]{1,0:T(8,128)}), (f32[16,512]{1,0:T(8,128)}, f32[16,512]{1,0:T(8,128)}, f32[16,512]{1,0:T(8,128)}, f32[16,512]{1,0:T(8,128)})) %all-reduce.12.cloned.1.call-update) | async-done | bytes 131088 | tf_op jit(solution)/shard_map/psum | solution.py:49
  (1493 shorter events, 301.2 us)
Async XLA Ops:
  6.5 729.2 %copy-start = (bf16[64,2048]{1,0:T(8,128)(2,1)S(1)}, bf16[64,2048]{1,0:T(8,128)(2,1)}, u32[]{:S(2)}) copy-start(bf16[64,2048]{1,0:T(8,128)(2,1)} %param.43) | copy-start | bytes 786436
  6.5 184.2 %copy-start.14 = (s32[16]{0:T(128)S(1)}, s32[16]{0:T(128)}, u32[]{:S(2)}) copy-start(s32[16]{0:T(128)} %param.51) | copy-start | bytes 196
  6.5 184.2 %copy-start.7 = (s32[16]{0:T(128)S(1)}, s32[16]{0:T(128)}, u32[]{:S(2)}) copy-start(s32[16]{0:T(128)} %param.52) | copy-start | bytes 196
  6.5 184.2 %copy-start.15 = (s32[16]{0:T(128)S(1)}, s32[16]{0:T(128)}, u32[]{:S(2)}) copy-start(s32[16]{0:T(128)} %param.53) | copy-start | bytes 196
  6.5 170.2 %all-reduce.18.cloned.1.call-start = ((), (), s32[]{:S(2)}) async-start(), calls=%async_computation.7 | async-start | bytes 786432 | tf_op jit(solution)/shard_map/psum | solution.py:49
  71.0 415.7 %all-gather.27.cloned.1.call-start = ((), (), s32[]{:S(2)}) async-start(), calls=%async_computation.3 | async-start | bytes 1081344 | tf_op jit(solution)/shard_map/all_gather | solution.py:19
  217.1 0.6 copy-start.11
  217.7 283.7 %all-gather.25.cloned.1.call-start = ((), (), s32[]{:S(2)}) async-start(), calls=%async_computation.2 | async-start | bytes 1081344 | tf_op jit(solution)/shard_map/all_gather | solution.py:19
  244.5 0.6 copy-start.10
  271.4 0.6 copy-start.9
  271.5 253.9 %all-gather.23.cloned.1.call-start = ((), (), s32[]{:S(2)}) async-start(), calls=%async_computation.1 | async-start | bytes 1081344 | tf_op jit(solution)/shard_map/all_gather | solution.py:19
  298.4 187.8 %copy-start.8 = (f32[1,16,4,128]{3,1,2,0:T(8,128)}, f32[1,16,4,128]{3,1,2,0:T(8,128)S(1)}, u32[]{:S(2)}) copy-start(f32[1,16,4,128]{3,1,2,0:T(8,128)S(1)} %get-tuple-element.921) | copy-start | bytes 98308
  461.3 42.3 %copy-start.4 = (f32[32,16,4]{1,2,0:T(4,128)}, f32[32,16,4]{1,2,0:T(4,128)S(1)}, u32[]{:S(2)}) copy-start(f32[32,16,4]{1,2,0:T(4,128)S(1)} %all-gather.1) | copy-start | bytes 24580
  485.4 18.3 %copy-start.5 = (f32[32,16,4]{1,2,0:T(4,128)}, f32[32,16,4]{1,2,0:T(4,128)S(1)}, u32[]{:S(2)}) copy-start(f32[32,16,4]{1,2,0:T(4,128)S(1)} %all-gather.2) | copy-start | bytes 24580
  485.9 94.0 %all-gather.21.cloned.1.call-start = ((), (), s32[]{:S(2)}) async-start(), calls=%async_computation | async-start | bytes 1081344 | tf_op jit(solution)/shard_map/all_gather | solution.py:19
  486.5 222.2 %all-reduce.14.cloned.1.call-start = ((), (), s32[]{:S(2)}) async-start(), calls=%async_computation.5 | async-start | bytes 262144 | tf_op jit(solution)/shard_map/psum | solution.py:49
  502.3 75.2 %copy-start.3 = (bf16[64,512]{1,0:T(8,128)(2,1)S(1)}, bf16[64,512]{1,0:T(8,128)(2,1)}, u32[]{:S(2)}) copy-start(bf16[64,512]{1,0:T(8,128)(2,1)} %param.41) | copy-start | bytes 196612
  515.9 66.0 %slice-start = ((f32[32,16,4]{1,2,0:T(4,128)}), f32[1,16,4]{1,2,0:T(4,128)S(1)}, s32[]{:S(2)}) async-start(f32[32,16,4]{1,2,0:T(4,128)} %copy-done.4), calls=%async_computation.8 | async-start | bytes 4096 | tf_op jit(solution)/shard_map/slice | solution.py:20
  515.9 66.0 %slice-start.1 = ((f32[32,16,4]{1,2,0:T(4,128)}), f32[1,16,4]{1,2,0:T(4,128)S(1)}, s32[]{:S(2)}) async-start(f32[32,16,4]{1,2,0:T(4,128)} %copy-done.5), calls=%async_computation.9 | async-start | bytes 4096 | tf_op jit(solution)/shard_map/slice | solution.py:20
  526.2 196.7 %copy-start.6 = (bf16[4,16,512]{2,1,0:T(8,128)(2,1)S(1)}, bf16[4,16,512]{2,1,0:T(8,128)(2,1)}, u32[]{:S(2)}) copy-start(bf16[4,16,512]{2,1,0:T(8,128)(2,1)} %param.37) | copy-start | bytes 196612
  526.2 196.7 %copy-start.12 = (f32[512]{0:T(512)S(1)}, f32[512]{0:T(512)}, u32[]{:S(2)}) copy-start(f32[512]{0:T(512)} %param.47) | copy-start | bytes 6148
  527.6 208.4 %copy-start.1 = (bf16[64,2048]{1,0:T(8,128)(2,1)S(1)}, bf16[64,2048]{1,0:T(8,128)(2,1)}, u32[]{:S(2)}) copy-start(bf16[64,2048]{1,0:T(8,128)(2,1)} %param.42) | copy-start | bytes 786436
  607.4 272.0 %all-reduce.16.cloned.1.call-start = ((), (), s32[]{:S(2)}) async-start(), calls=%async_computation.6 | async-start | bytes 2097152 | tf_op jit(solution)/shard_map/psum | solution.py:49
  709.5 197.2 %copy-start.2 = (bf16[256,512]{1,0:T(8,128)(2,1)S(1)}, bf16[256,512]{1,0:T(8,128)(2,1)}, u32[]{:S(2)}) copy-start(bf16[256,512]{1,0:T(8,128)(2,1)} %param.44) | copy-start | bytes 786436
  760.8 289.7 %copy-start.13 = (f32[512]{0:T(512)S(1)}, f32[512]{0:T(512)}, u32[]{:S(2)}) copy-start(f32[512]{0:T(512)} %param.48) | copy-start | bytes 6148
  776.2 260.1 %all-reduce.12.cloned.1.call-start = ((), (), s32[]{:S(2)}) async-start(), calls=%async_computation.4 | async-start | bytes 262144 | tf_op jit(solution)/shard_map/psum | solution.py:49
Sparse Core Ops, SparseCore 0:
  71.1 105.5 all-reduce.17
  217.9 38.5 all-gather.26
  271.6 38.4 all-gather.24
  486.0 39.4 all-gather.22
  527.5 41.8 all-gather.20
  607.5 101.1 all-reduce.13
  776.3 102.9 all-reduce.15
  936.5 99.7 all-reduce.11
where the time goes:
time: 1060 us
  waiting for transfers between devices  419 us (40%)
  blocking collectives  408 us (38%)
  local copies, waits for them, and re-layouts  86.7 us (8%)
  other arithmetic  64.3 us (6%)
  matrix products  60.5 us (6%)
  between operations  14.4 us (1%)
    psum x4, waiting for transfers between devices, seq_total(): return lax.psum(partial_value, 'seq')  409 us
    all_gather x16, blocking collectives, seq_columns(): gathered = lax.all_gather(token_rows, 'mp', axis=1, tiled=True)  194 us
    all_gather x8, blocking collectives, combined_all(): pieces = jax.tree.map(lambda part: lax.all_gather(part, axis), value)  182 us
    psum x3, blocking collectives, feature_sums(): return lax.psum(squares, 'mp')  32 us
    dot_general x16, matrix products, fold_block(): jnp.einsum('sghd,gthd->sgth', picked, key_block, preferred_element_type=j...  25.3 us
  transfers between devices with their start and end apart: 8, of which 5 were waited for; matrix products, arithmetic and copies ran while one was open for 12% of the time, Pallas kernels for 0%

commit v1 on v0

--- a/solution.py
+++ b/solution.py
@@ -41,7 +41,22 @@
 
 
 def seq_columns(token_rows, width):
-    gathered = lax.all_gather(token_rows, "mp", axis=1, tiled=True)
+    dev_n = lax.psum(1, axis_name="mp")
+    table = []
+    for t in range(dev_n):
+        table.append((t, (t + 1) % dev_n))
+    nodes = []
+    for t in range(dev_n):
+        nodes.append((t, (t - 1) % dev_n))
+    n_now, y2 = ([token_rows], [token_rows])
+    for _ in range(dev_n // 2):
+        n_now.append(lax.ppermute(n_now[-1], axis_name="mp", perm=table))
+    for _ in range((dev_n - 1) // 2):
+        y2.append(lax.ppermute(y2[-1], perm=nodes, axis_name="mp"))
+    part_now = jnp.concatenate([*n_now[::-1], *y2[1:]], axis=1)
+    gathered = jnp.roll(
+        part_now, shift=(lax.axis_index("mp") - dev_n // 2) * token_rows.shape[1], axis=1
+    )
     return lax.dynamic_slice_in_dim(gathered, lax.axis_index("seq") * width, width, 1)
 
 

time: 1060 us -> 968 us (0.913)
  blocking collectives: 408 us -> 215 us
  starting transfers between devices: 0.51 us -> 57.9 us
  waiting for transfers between devices: 419 us -> 459 us
    all_gather x16 -> x0, blocking collectives: 194 us -> none  [seq_columns(): gathered = lax.all_gather(token_rows, 'mp', axis=1, tiled=True)]
    ppermute x0 -> x48, starting transfers between devices: none -> 57.3 us  [the longest x16 43.9 us: seq_columns(): y2.append(lax.ppermute(y2[-1], perm=nodes, axis_name='mp'))]
    ppermute x0 -> x48, waiting for transfers between devices: none -> 21 us  [the longest x32 21 us: seq_columns(): n_now.append(lax.ppermute(n_now[-1], axis_name='mp', perm=table))]
    all_gather x4, waiting for transfers between devices: 9.29 us -> 30.2 us  [combined_all(): pieces = jax.tree.map(lambda part: lax.all_gather(part, axis), value)]
  transfers between devices with their start and end apart: 8 -> 56, of which waited for: 5 -> 19; matrix products, arithmetic and copies ran while one was open for 12% -> 17% of each run, Pallas kernels for 0% -> 0%
where the time goes in v1:
time: 968 us; the launch traced here: 964 us
  waiting for transfers between devices  459 us (47%)
  blocking collectives  215 us (22%)
  local copies, waits for them, and re-layouts  86.8 us (9%)
  other arithmetic  65 us (7%)
  matrix products  61.1 us (6%)
  starting transfers between devices  57.9 us (6%)
  between operations  14.6 us (2%)
    psum x4, waiting for transfers between devices, seq_total(): return lax.psum(partial_value, 'seq')  407 us
    all_gather x8, blocking collectives, combined_all(): pieces = jax.tree.map(lambda part: lax.all_gather(part, axis), value)  182 us
    ppermute x16, starting transfers between devices, seq_columns(): y2.append(lax.ppermute(y2[-1], perm=nodes, axis_name='mp'))  43.9 us
    psum x3, blocking collectives, feature_sums(): return lax.psum(squares, 'mp')  32 us
    all_gather x4, waiting for transfers between devices, combined_all(): pieces = jax.tree.map(lambda part: lax.all_gather(part, axis), value)  30.2 us
    dot_general x16, matrix products, fold_block(): jnp.einsum('sghd,gthd->sgth', picked, key_block, preferred_element_type=j...  25.3 us
    dynamic_slice x16, local copies, waits for them, and re-layouts, fold_block(): lax.dynamic_slice_in_dim(value_cache, first_page, pages_per_block, 0)  21.1 us
    ppermute x32, waiting for transfers between devices, seq_columns(): n_now.append(lax.ppermute(n_now[-1], axis_name='mp', perm=table))  21 us
  transfers between devices with their start and end apart: 56, of which 19 were waited for; matrix products, arithmetic and copies ran while one was open for 17% of the time, Pallas kernels for 0%

profile of v1, /device:TPU:6, one launch (start us, length us, event | category | flops | bytes accessed | tf_op | source)
XLA Modules:
  0.0 964.4 jit_solution(4742902132112001146)
XLA Ops:
  7.4 4.0 collective-permute-start.2
  20.4 3.3 collective-permute-done.1
  42.9 106.3 %all-reduce.18.cloned.1.call-done = (f32[16,1536]{1,0:T(8,128)}, f32[16,1536]{1,0:T(8,128)}, f32[16,1536]{1,0:T(8,128)}, f32[16,1536]{1,0:T(8,128)}) async-done(((f32[16,1536]{1,0:T(8,128)}, f32[16,1536]{1,0:T(8,128)}, f32[16,1536]{1,0:T(8,128)}, f32[16,1536]{1,0:T(8,128)}), (f32[16,1536]{1,0:T(8,128)}, f32[16,1536]{1,0:T(8,128)}, f32[16,1536]{1,0:T(8,128)}, ...) | async-done | bytes 393232 | tf_op jit(solution)/shard_map/psum | solution.py:64
  151.2 10.7 %all-reduce.6 = (f32[16,2]{0,1:T(2,128)S(1)}, f32[16,2]{0,1:T(2,128)S(1)}, f32[16,2]{0,1:T(2,128)S(1)}, f32[16,2]{0,1:T(2,128)S(1)}) all-reduce(f32[16,2]{0,1:T(2,128)S(1)} %pad_maximum_fusion.19, f32[16,2]{0,1:T(2,128)S(1)} %pad_maximum_fusion.18, f32[16,2]{0,1:T(2,128)S(1)} %pad_maximum_fusion.17, ...), channel_id=1, replica_groups=mesh['seq'=32,'mp'=4] {'mp'}, use_global_device_ids=true, to_apply=%region_64.69 | all-reduce | flops 128 | bytes 1024 | tf_op jit(solution)/shard_map/psum | solution.py:68
  163.3 26.4 %while.139 = (s32[]{:T(128)}, f32[1,16,4]{1,2,0:T(4,128)S(1)}, f32[1,16,4]{1,2,0:T(4,128)S(1)}, f32[1,16,4,128]{3,1,2,0:T(8,128)S(1)}, s32[16]{0:T(128)S(1)}, /*...) while((s32[]{:T(128)}, f32[1,16,4]{1,2,0:T(4,128)S(1)}, ...), condition=%wide.region_70.75_spmd.clone.clone, body=%wide.region_65.74_spmd.clone.clone.sunk | while | flops 2561347 | bytes 6471395 | solution.py:201
  190.6 26.4 %while.138 = (s32[]{:T(128)}, f32[1,16,4]{1,2,0:T(4,128)S(1)}, f32[1,16,4]{1,2,0:T(4,128)S(1)}, f32[1,16,4,128]{3,1,2,0:T(8,128)S(1)}, s32[16]{0:T(128)S(1)}, /*...) while((s32[]{:T(128)}, f32[1,16,4]{1,2,0:T(4,128)S(1)}, ...), condition=%wide.region_49.54_spmd.clone.clone, body=%wide.region_44.53_spmd.clone.clone.sunk | while | flops 2561347 | bytes 6471395 | solution.py:201
  217.6 26.3 %while.137 = (s32[]{:T(128)}, f32[1,16,4]{1,2,0:T(4,128)S(1)}, f32[1,16,4]{1,2,0:T(4,128)S(1)}, f32[1,16,4,128]{3,1,2,0:T(8,128)S(1)}, s32[16]{0:T(128)S(1)}, /*...) while((s32[]{:T(128)}, f32[1,16,4]{1,2,0:T(4,128)S(1)}, ...), condition=%wide.region_28.33_spmd.clone.clone, body=%wide.region_23.32_spmd.clone.clone.sunk | while | flops 2561347 | bytes 6471395 | solution.py:201
  244.6 26.4 %while.136 = (s32[]{:T(128)}, f32[1,16,4]{1,2,0:T(4,128)S(1)}, f32[1,16,4]{1,2,0:T(4,128)S(1)}, f32[1,16,4,128]{3,1,2,0:T(8,128)S(1)}, s32[16]{0:T(128)S(1)}, /*...) while((s32[]{:T(128)}, f32[1,16,4]{1,2,0:T(4,128)S(1)}, ...), condition=%wide.region_9.13_spmd.clone.clone, body=%wide.region_4.12_spmd.clone.clone.sunk | while | flops 2561347 | bytes 6471395 | solution.py:201
  274.0 21.3 %all-gather.9 = f32[32,16,4]{1,2,0:T(4,128)S(1)} all-gather(f32[1,16,4]{1,2,0:T(4,128)S(1)} %get-tuple-element.939), channel_id=11, replica_groups=mesh['seq'=32,'mp'=4] {'seq'}, dimensions={0}, use_global_device_ids=true | all-gather | bytes 8448 | tf_op jit(solution)/shard_map/all_gather | solution.py:19
  295.4 24.4 %all-gather.10 = f32[32,16,4]{1,2,0:T(4,128)S(1)} all-gather(f32[1,16,4]{1,2,0:T(4,128)S(1)} %get-tuple-element.940), channel_id=12, replica_groups=mesh['seq'=32,'mp'=4] {'seq'}, dimensions={0}, use_global_device_ids=true | all-gather | bytes 8448 | tf_op jit(solution)/shard_map/all_gather | solution.py:19
  320.4 21.6 %all-gather.6 = f32[32,16,4]{1,2,0:T(4,128)S(1)} all-gather(f32[1,16,4]{1,2,0:T(4,128)S(1)} %get-tuple-element.933), channel_id=8, replica_groups=mesh['seq'=32,'mp'=4] {'seq'}, dimensions={0}, use_global_device_ids=true | all-gather | bytes 8448 | tf_op jit(solution)/shard_map/all_gather | solution.py:19
  342.0 24.0 %all-gather.7 = f32[32,16,4]{1,2,0:T(4,128)S(1)} all-gather(f32[1,16,4]{1,2,0:T(4,128)S(1)} %get-tuple-element.934), channel_id=9, replica_groups=mesh['seq'=32,'mp'=4] {'seq'}, dimensions={0}, use_global_device_ids=true | all-gather | bytes 8448 | tf_op jit(solution)/shard_map/all_gather | solution.py:19
  366.5 21.6 %all-gather.3 = f32[32,16,4]{1,2,0:T(4,128)S(1)} all-gather(f32[1,16,4]{1,2,0:T(4,128)S(1)} %get-tuple-element.927), channel_id=5, replica_groups=mesh['seq'=32,'mp'=4] {'seq'}, dimensions={0}, use_global_device_ids=true | all-gather | bytes 8448 | tf_op jit(solution)/shard_map/all_gather | solution.py:19
  388.0 24.0 %all-gather.4 = f32[32,16,4]{1,2,0:T(4,128)S(1)} all-gather(f32[1,16,4]{1,2,0:T(4,128)S(1)} %get-tuple-element.928), channel_id=6, replica_groups=mesh['seq'=32,'mp'=4] {'seq'}, dimensions={0}, use_global_device_ids=true | all-gather | bytes 8448 | tf_op jit(solution)/shard_map/all_gather | solution.py:19
  412.5 21.6 %all-gather = f32[32,16,4]{1,2,0:T(4,128)S(1)} all-gather(f32[1,16,4]{1,2,0:T(4,128)S(1)} %get-tuple-element.921), channel_id=2, replica_groups=mesh['seq'=32,'mp'=4] {'seq'}, dimensions={0}, use_global_device_ids=true | all-gather | bytes 8448 | tf_op jit(solution)/shard_map/all_gather | solution.py:19
  434.1 24.0 %all-gather.1 = f32[32,16,4]{1,2,0:T(4,128)S(1)} all-gather(f32[1,16,4]{1,2,0:T(4,128)S(1)} %get-tuple-element.922), channel_id=3, replica_groups=mesh['seq'=32,'mp'=4] {'seq'}, dimensions={0}, use_global_device_ids=true | all-gather | bytes 8448 | tf_op jit(solution)/shard_map/all_gather | solution.py:19
  461.3 12.3 %while.135 = (s32[]{:T(128)}, f32[1,16,4]{1,2,0:T(4,128)S(1)}, f32[1,16,4]{1,2,0:T(4,128)S(1)}, f32[1,16,4,128]{3,2,1,0:T(4,128)S(1)}, f32[31,1,16,4]{2,3,1,0:T(...) while((s32[]{:T(128)}, f32[1,16,4]{1,2,0:T(4,128)S(1)}, ...), condition=%wide.region_72.77_spmd, body=%wide.region_71.76_spmd.sunk | while | flops 25026 | bytes 168809 | solution.py:22
  478.6 12.3 %while.134 = (s32[]{:T(128)}, f32[1,16,4]{1,2,0:T(4,128)S(1)}, f32[1,16,4]{1,2,0:T(4,128)S(1)}, f32[1,16,4,128]{3,2,1,0:T(4,128)S(1)}, f32[31,1,16,4]{2,3,1,0:T(...) while((s32[]{:T(128)}, f32[1,16,4]{1,2,0:T(4,128)S(1)}, ...), condition=%wide.region_51.56_spmd, body=%wide.region_50.55_spmd.sunk | while | flops 25026 | bytes 168809 | solution.py:22
  493.7 4.5 all-gather.19.cloned.1.call-done
  500.4 12.3 %while.133 = (s32[]{:T(128)}, f32[1,16,4]{1,2,0:T(4,128)S(1)}, f32[1,16,4]{1,2,0:T(4,128)S(1)}, f32[1,16,4,128]{3,2,1,0:T(4,128)S(1)}, f32[31,1,16,4]{2,3,1,0:T(...) while((s32[]{:T(128)}, f32[1,16,4]{1,2,0:T(4,128)S(1)}, ...), condition=%wide.region_30.35_spmd, body=%wide.region_29.34_spmd.sunk | while | flops 25026 | bytes 168809 | solution.py:22
  516.4 25.8 %all-gather.17.cloned.1.call-done = f32[32,16,4,128]{3,1,2,0:T(8,128)} async-done(((f32[1,16,4,128]{3,1,2,0:T(8,128)}), f32[32,16,4,128]{3,1,2,0:T(8,128)}) %all-gather.17.cloned.1.call-update) | async-done | bytes 1048592 | tf_op jit(solution)/shard_map/all_gather | solution.py:19
  544.3 12.3 %while.132 = (s32[]{:T(128)}, f32[1,16,4]{1,2,0:T(4,128)S(1)}, f32[1,16,4]{1,2,0:T(4,128)S(1)}, f32[1,16,4,128]{3,2,1,0:T(4,128)S(1)}, f32[31,1,16,4]{2,3,1,0:T(...) while((s32[]{:T(128)}, f32[1,16,4]{1,2,0:T(4,128)S(1)}, ...), condition=%wide.region_11.15_spmd, body=%wide.region_10.14_spmd.sunk | while | flops 25026 | bytes 168809 | solution.py:22
  567.6 3.2 collective-permute-done.16
  572.9 99.7 %all-reduce.14.cloned.1.call-done = (f32[16,512]{1,0:T(8,128)}, f32[16,512]{1,0:T(8,128)}, f32[16,512]{1,0:T(8,128)}, f32[16,512]{1,0:T(8,128)}) async-done(((f32[16,512]{1,0:T(8,128)}, f32[16,512]{1,0:T(8,128)}, f32[16,512]{1,0:T(8,128)}, f32[16,512]{1,0:T(8,128)}), (f32[16,512]{1,0:T(8,128)}, f32[16,512]{1,0:T(8,128)}, f32[16,512]{1,0:T(8,128)}, f32[16,512]{1,0:T(8,128)})) %all-reduce.14.cloned.1.call-update) | async-done | bytes 131088 | tf_op jit(solution)/shard_map/psum | solution.py:64
  676.1 10.7 %all-reduce.5 = (f32[16,1]{0,1:T(1,128)S(1)}, f32[16,1]{0,1:T(1,128)S(1)}, f32[16,1]{0,1:T(1,128)S(1)}, f32[16,1]{0,1:T(1,128)S(1)}) all-reduce(f32[16,1]{0,1:T(1,128)S(1)} %bitcast.1045, f32[16,1]{0,1:T(1,128)S(1)} %bitcast.1046, f32[16,1]{0,1:T(1,128)S(1)} %bitcast.1047, ...), channel_id=1, replica_groups=mesh['seq'=32,'mp'=4] {'mp'}, use_global_device_ids=true, to_apply=%region_77.82 | all-reduce | flops 64 | bytes 512 | tf_op jit(solution)/shard_map/psum | solution.py:68
  710.4 102.7 %all-reduce.16.cloned.1.call-done = (f32[16,4096]{1,0:T(8,128)}, f32[16,4096]{1,0:T(8,128)}, f32[16,4096]{1,0:T(8,128)}, f32[16,4096]{1,0:T(8,128)}) async-done(((f32[16,4096]{1,0:T(8,128)}, f32[16,4096]{1,0:T(8,128)}, f32[16,4096]{1,0:T(8,128)}, f32[16,4096]{1,0:T(8,128)}), (f32[16,4096]{1,0:T(8,128)}, f32[16,4096]{1,0:T(8,128)}, f32[16,4096]{1,0:T(8,128)}, ...) | async-done | bytes 1048592 | tf_op jit(solution)/shard_map/psum | solution.py:64
  818.1 3.3 collective-permute-start.35
  822.4 3.3 collective-permute-start.23
  828.4 3.3 collective-permute-done.46
  838.0 3.2 collective-permute-done.22
  843.1 98.7 %all-reduce.12.cloned.1.call-done = (f32[16,512]{1,0:T(8,128)}, f32[16,512]{1,0:T(8,128)}, f32[16,512]{1,0:T(8,128)}, f32[16,512]{1,0:T(8,128)}) async-done(((f32[16,512]{1,0:T(8,128)}, f32[16,512]{1,0:T(8,128)}, f32[16,512]{1,0:T(8,128)}, f32[16,512]{1,0:T(8,128)}), (f32[16,512]{1,0:T(8,128)}, f32[16,512]{1,0:T(8,128)}, f32[16,512]{1,0:T(8,128)}, f32[16,512]{1,0:T(8,128)})) %all-reduce.12.cloned.1.call-update) | async-done | bytes 131088 | tf_op jit(solution)/shard_map/psum | solution.py:64
  945.3 10.7 %all-reduce.4 = (f32[16,1]{0,1:T(1,128)S(1)}, f32[16,1]{0,1:T(1,128)S(1)}, f32[16,1]{0,1:T(1,128)S(1)}, f32[16,1]{0,1:T(1,128)S(1)}) all-reduce(f32[16,1]{0,1:T(1,128)S(1)} %bitcast.1048, f32[16,1]{0,1:T(1,128)S(1)} %bitcast.1049, f32[16,1]{0,1:T(1,128)S(1)} %bitcast.1050, ...), channel_id=1, replica_groups=mesh['seq'=32,'mp'=4] {'mp'}, use_global_device_ids=true, to_apply=%region_81.86 | all-reduce | flops 64 | bytes 512 | tf_op jit(solution)/shard_map/psum | solution.py:68
  (1577 shorter events, 268.4 us)
Async XLA Ops:
  6.5 142.7 %all-reduce.18.cloned.1.call-start = ((), (), s32[]{:S(2)}) async-start(), calls=%async_computation.7 | async-start | bytes 786432 | tf_op jit(solution)/shard_map/psum | solution.py:64
  7.4 11.5 %collective-permute-start.2 = (bf16[16,512]{1,0:T(8,128)(2,1)S(1)}, bf16[16,512]{1,0:T(8,128)(2,1)S(1)}, u32[]{:S(2)}, u32[]{:S(2)}) collective-permute-start(bf16[16,512]{1,0:T(8,128)(2,1)S(1)} %get-tuple-element.1526), channel_id=1, source_target_pairs={{0,3},{1,0},{2,1},{3,2},{4,7},{5,4},{6,5},{7,6},{8,11},{9,8},{10,9... | collective-permute-start | bytes 49160 | tf_op jit(solution)/shard_map/ppermute | solution.py:55
  11.4 14.3 %collective-permute-start.38 = (bf16[16,512]{1,0:T(8,128)(2,1)S(1)}, bf16[16,512]{1,0:T(8,128)(2,1)S(1)}, u32[]{:S(2)}, u32[]{:S(2)}) collective-permute-start(bf16[16,512]{1,0:T(8,128)(2,1)S(1)} %get-tuple-element.1527), channel_id=1, source_target_pairs={{0,3},{1,0},{2,1},{3,2},{4,7},{5,4},{6,5},{7,6},{8,11},{9,8},{10,9... | collective-permute-start | bytes 49160 | tf_op jit(solution)/shard_map/ppermute | solution.py:55
  14.7 18.4 %collective-permute-start.26 = (bf16[16,512]{1,0:T(8,128)(2,1)S(1)}, bf16[16,512]{1,0:T(8,128)(2,1)S(1)}, u32[]{:S(2)}, u32[]{:S(2)}) collective-permute-start(bf16[16,512]{1,0:T(8,128)(2,1)S(1)} %get-tuple-element.1528), channel_id=1, source_target_pairs={{0,3},{1,0},{2,1},{3,2},{4,7},{5,4},{6,5},{7,6},{8,11},{9,8},{10,9... | collective-permute-start | bytes 49160 | tf_op jit(solution)/shard_map/ppermute | solution.py:55
  18.9 10.1 %collective-permute-start.24 = (bf16[16,512]{1,0:T(8,128)(2,1)S(1)}, bf16[16,512]{1,0:T(8,128)(2,1)S(1)}, u32[]{:S(2)}, u32[]{:S(2)}) collective-permute-start(bf16[16,512]{1,0:T(8,128)(2,1)S(1)} %get-tuple-element.1528), channel_id=1, source_target_pairs={{0,1},{1,2},{2,3},{3,0},{4,5},{5,6},{6,7},{7,4},{8,9},{9,10},{10,1... | collective-permute-start | bytes 49160 | tf_op jit(solution)/shard_map/ppermute | solution.py:53
  19.6 9.4 collective-permute-start.12
  25.8 11.2 %collective-permute-start.14 = (bf16[16,512]{1,0:T(8,128)(2,1)S(1)}, bf16[16,512]{1,0:T(8,128)(2,1)S(1)}, u32[]{:S(2)}, u32[]{:S(2)}) collective-permute-start(bf16[16,512]{1,0:T(8,128)(2,1)S(1)} %get-tuple-element.1525), channel_id=1, source_target_pairs={{0,3},{1,0},{2,1},{3,2},{4,7},{5,4},{6,5},{7,6},{8,11},{9,8},{10,9... | collective-permute-start | bytes 49160 | tf_op jit(solution)/shard_map/ppermute | solution.py:55
  29.0 8.0 collective-permute-start.13
  42.6 416.6 %all-gather.23.cloned.1.call-start = ((), (), s32[]{:S(2)}) async-start(), calls=%async_computation.3 | async-start | bytes 1081344 | tf_op jit(solution)/shard_map/all_gather | solution.py:19
  190.3 286.2 %all-gather.21.cloned.1.call-start = ((), (), s32[]{:S(2)}) async-start(), calls=%async_computation.2 | async-start | bytes 1081344 | tf_op jit(solution)/shard_map/all_gather | solution.py:19
  244.0 254.2 %all-gather.19.cloned.1.call-start = ((), (), s32[]{:S(2)}) async-start(), calls=%async_computation.1 | async-start | bytes 1081344 | tf_op jit(solution)/shard_map/all_gather | solution.py:19
  458.6 83.6 %all-gather.17.cloned.1.call-start = ((), (), s32[]{:S(2)}) async-start(), calls=%async_computation | async-start | bytes 1081344 | tf_op jit(solution)/shard_map/all_gather | solution.py:19
  459.2 213.4 %all-reduce.14.cloned.1.call-start = ((), (), s32[]{:S(2)}) async-start(), calls=%async_computation.5 | async-start | bytes 262144 | tf_op jit(solution)/shard_map/psum | solution.py:64
  474.4 84.1 %collective-permute-start.41 = (bf16[16,512]{1,0:T(8,128)(2,1)S(1)}, bf16[16,512]{1,0:T(8,128)(2,1)S(1)}, u32[]{:S(2)}, u32[]{:S(2)}) collective-permute-start(bf16[16,512]{1,0:T(8,128)(2,1)S(1)} %bitcast.1026), channel_id=1, source_target_pairs={{0,3},{1,0},{2,1},{3,2},{4,7},{5,4},{6,5},{7,6},{8,11},{9,8},{10,9... | collective-permute-start | bytes 49160 | tf_op jit(solution)/shard_map/ppermute | solution.py:55
  474.5 82.4 %collective-permute-start.39 = (bf16[16,512]{1,0:T(8,128)(2,1)S(1)}, bf16[16,512]{1,0:T(8,128)(2,1)S(1)}, u32[]{:S(2)}, u32[]{:S(2)}) collective-permute-start(bf16[16,512]{1,0:T(8,128)(2,1)S(1)} %bitcast.1027), channel_id=1, source_target_pairs={{0,1},{1,2},{2,3},{3,0},{4,5},{5,6},{6,7},{7,4},{8,9},{9,10},{10,1... | collective-permute-start | bytes 49160 | tf_op jit(solution)/shard_map/ppermute | solution.py:53
  491.6 71.4 %collective-permute-start.29 = (bf16[16,512]{1,0:T(8,128)(2,1)S(1)}, bf16[16,512]{1,0:T(8,128)(2,1)S(1)}, u32[]{:S(2)}, u32[]{:S(2)}) collective-permute-start(bf16[16,512]{1,0:T(8,128)(2,1)S(1)} %bitcast.1029), channel_id=1, source_target_pairs={{0,3},{1,0},{2,1},{3,2},{4,7},{5,4},{6,5},{7,6},{8,11},{9,8},{10,9... | collective-permute-start | bytes 49160 | tf_op jit(solution)/shard_map/ppermute | solution.py:55
  493.0 67.2 %collective-permute-start.27 = (bf16[16,512]{1,0:T(8,128)(2,1)S(1)}, bf16[16,512]{1,0:T(8,128)(2,1)S(1)}, u32[]{:S(2)}, u32[]{:S(2)}) collective-permute-start(bf16[16,512]{1,0:T(8,128)(2,1)S(1)} %bitcast.1030), channel_id=1, source_target_pairs={{0,1},{1,2},{2,3},{3,0},{4,5},{5,6},{6,7},{7,4},{8,9},{9,10},{10,1... | collective-permute-start | bytes 49160 | tf_op jit(solution)/shard_map/ppermute | solution.py:53
  513.4 54.2 %collective-permute-start.17 = (bf16[16,512]{1,0:T(8,128)(2,1)S(1)}, bf16[16,512]{1,0:T(8,128)(2,1)S(1)}, u32[]{:S(2)}, u32[]{:S(2)}) collective-permute-start(bf16[16,512]{1,0:T(8,128)(2,1)S(1)} %bitcast.1032), channel_id=1, source_target_pairs={{0,3},{1,0},{2,1},{3,2},{4,7},{5,4},{6,5},{7,6},{8,11},{9,8},{10,9... | collective-permute-start | bytes 49160 | tf_op jit(solution)/shard_map/ppermute | solution.py:55
  558.5 7.4 collective-permute-start.15
  563.0 8.7 collective-permute-start.5
  572.6 240.5 %all-reduce.16.cloned.1.call-start = ((), (), s32[]{:S(2)}) async-start(), calls=%async_computation.6 | async-start | bytes 2097152 | tf_op jit(solution)/shard_map/psum | solution.py:64
  687.8 8.5 collective-permute-start.44
  696.0 9.7 %collective-permute-start.20 = (bf16[16,512]{1,0:T(8,128)(2,1)S(1)}, bf16[16,512]{1,0:T(8,128)(2,1)S(1)}, u32[]{:S(2)}, u32[]{:S(2)}) collective-permute-start(bf16[16,512]{1,0:T(8,128)(2,1)S(1)} %get-tuple-element.1522), channel_id=1, source_target_pairs={{0,3},{1,0},{2,1},{3,2},{4,7},{5,4},{6,5},{7,6},{8,11},{9,8},{10,9... | collective-permute-start | bytes 49160 | tf_op jit(solution)/shard_map/ppermute | solution.py:55
  699.5 9.4 collective-permute-start.8
  710.3 231.5 %all-reduce.12.cloned.1.call-start = ((), (), s32[]{:S(2)}) async-start(), calls=%async_computation.4 | async-start | bytes 262144 | tf_op jit(solution)/shard_map/psum | solution.py:64
  814.1 12.7 %collective-permute-start.47 = (bf16[16,2048]{1,0:T(8,128)(2,1)S(1)}, bf16[16,2048]{1,0:T(8,128)(2,1)S(1)}, u32[]{:S(2)}, u32[]{:S(2)}) collective-permute-start(bf16[16,2048]{1,0:T(8,128)(2,1)S(1)} %fusion.120), channel_id=1, source_target_pairs={{0,3},{1,0},{2,1},{3,2},{4,7},{5,4},{6,5},{7,6},{8,11},{9,8},{10,9... | collective-permute-start | bytes 196616 | tf_op jit(solution)/shard_map/ppermute | solution.py:55
  817.1 8.6 collective-permute-start.45
  818.1 14.4 %collective-permute-start.35 = (bf16[16,2048]{1,0:T(8,128)(2,1)S(1)}, bf16[16,2048]{1,0:T(8,128)(2,1)S(1)}, u32[]{:S(2)}, u32[]{:S(2)}) collective-permute-start(bf16[16,2048]{1,0:T(8,128)(2,1)S(1)} %fusion.121), channel_id=1, source_target_pairs={{0,3},{1,0},{2,1},{3,2},{4,7},{5,4},{6,5},{7,6},{8,11},{9,8},{10,9... | collective-permute-start | bytes 196616 | tf_op jit(solution)/shard_map/ppermute | solution.py:55
  822.4 15.6 %collective-permute-start.23 = (bf16[16,2048]{1,0:T(8,128)(2,1)S(1)}, bf16[16,2048]{1,0:T(8,128)(2,1)S(1)}, u32[]{:S(2)}, u32[]{:S(2)}) collective-permute-start(bf16[16,2048]{1,0:T(8,128)(2,1)S(1)} %fusion.122), channel_id=1, source_target_pairs={{0,3},{1,0},{2,1},{3,2},{4,7},{5,4},{6,5},{7,6},{8,11},{9,8},{10,9... | collective-permute-start | bytes 196616 | tf_op jit(solution)/shard_map/ppermute | solution.py:55
  826.8 9.0 collective-permute-start.21
  827.6 8.2 collective-permute-start.9
  832.5 9.6 collective-permute-start.11
  (42 other events, 2701.4 us)
Sparse Core Ops, SparseCore 0:
  42.8 106.4 all-reduce.17
  190.4 38.5 all-gather.22
  244.2 38.3 all-gather.20
  458.7 39.4 all-gather.18
  500.3 41.8 all-gather.16
  572.7 99.7 all-reduce.13
  710.4 102.5 all-reduce.15
  843.2 98.5 all-reduce.11
